TPU v7x, 256 devices: a whole 4x4x8 slice. The times are simulated.
256 devices in a mesh: shard: 64 (over y, z, core), cent: 4 (over x).
Axes of the slice: x: 4, y: 4, z: 8, core: 2. Of those that a mesh axis runs over, the one named last changes fastest.
Arguments:
- queries: bfloat16 [1024, 32, 128], P('shard'), may hold values from -6 to 6
- centroids: bfloat16 [196608, 128], P(('shard', 'cent')), may hold values from -0.5 to 0.5
- passages: bfloat16 [16384, 128, 128], P('shard', 'cent'), may hold values from -0.5 to 0.5
- lengths: int32 [16384], P('shard'), may hold values from 16 to 128, as said below
- passage_row: int32 [16384], replicated, may hold values from 0 to 16383, as said below
- candidates: int32 [1024, 16], P('shard'), may hold values from 0 to 16383, as said below
Outputs:
- token_best: float32 [1024, 32], P('shard')
- scores: float32 [1024, 16], P('shard')
Inputs may be any that keep to these rules, and one draw needn't show every extreme that they name: A permutation: passage g is stored at row passage_row[g]. The rows j < lengths[r] of stored passage r are real, the rest padding; the first stored passage of every index of shard has all 128. Among the 256 pairs of the queries of one index of shard, at most 12 have candidates stored at one owner (owner = passage_row[id] // 256); one owner takes exactly 12 pairs from every index of shard.
All inputs are finite; a program needn't handle non-finite values.
Results may differ from a plain program's by a relative error of at most 0.0003.
Values may be sent and summed in bfloat16 or wider, within the bound.
No kernel may reach another device: no remote copies, remote signals or barrier semaphores. Data moves between devices by JAX's collectives and lax.ppermute only.
A program may use at most 128 MiB of HBM per device.

v0:
```python
import jax
import jax.numpy as jnp
from jax import lax
from jax.sharding import PartitionSpec as P

masked_score = -1e30


def per_device(queries, centroids, passages, lengths, passage_row, candidates):
    query_count = queries.shape[0]
    query_tokens = queries.shape[1]
    feature_width = queries.shape[2]
    per_query = candidates.shape[1]
    passage_count = passages.shape[0]
    token_rows = passages.shape[1]
    shard_total = lax.axis_size("shard")
    capacity = max(2, 3 * query_count * per_query // shard_total)
    pairs_here = query_count * per_query
    my_shard = lax.axis_index("shard")
    query_block = lax.all_gather(queries, "shard", axis=0, tiled=True)
    cand_block = lax.all_gather(candidates, "shard", axis=0, tiled=True)
    flattened = query_block.reshape(-1, feature_width)
    scored = jnp.einsum("rd,cd->rc", flattened, centroids, preferred_element_type=jnp.float32)
    local_best = jnp.max(scored, axis=1).reshape(shard_total, query_count, query_tokens)
    gathered_best = lax.all_to_all(local_best, "shard", split_axis=0, concat_axis=0, tiled=True)
    shard_best = jnp.max(gathered_best, axis=0)
    all_rows = jnp.take(passage_row, cand_block.reshape(-1), axis=0)
    is_mine = (all_rows // passage_count == my_shard).reshape(shard_total, pairs_here)
    mine_int = is_mine.astype(jnp.int32)
    rank = jnp.cumsum(mine_int, axis=1) - mine_int
    source_ids = jnp.arange(shard_total, dtype=jnp.int32)[:, None]
    places = jnp.where(is_mine, source_ids * capacity + rank, shard_total * capacity).reshape(-1)
    pair_query = jnp.arange(shard_total * pairs_here, dtype=jnp.int32) // per_query
    slot_table = (
        jnp.zeros((shard_total * capacity,), jnp.int32)
        .at[places]
        .set(all_rows % passage_count, mode="drop")
    )
    query_table = (
        jnp.zeros((shard_total * capacity,), jnp.int32).at[places].set(pair_query, mode="drop")
    )
    asked = jnp.take(query_block, query_table, axis=0)
    chosen = jnp.take(passages, slot_table, axis=0)
    pair_scored = jnp.einsum("ntd,npd->ntp", asked, chosen, preferred_element_type=jnp.float32)
    token_index = lax.axis_index("cent") * token_rows + jnp.arange(token_rows, dtype=jnp.int32)
    valid_tokens = token_index[None, :] < jnp.take(lengths, slot_table, axis=0)[:, None]
    pair_scored = jnp.where(valid_tokens[:, None, :], pair_scored, masked_score)
    partial_value = jnp.max(pair_scored, axis=2)
    merged = lax.pmax(jnp.concatenate([shard_best, partial_value], axis=0), "cent")
    token_best = merged[:query_count]
    complete = merged[query_count:]
    pair_scores = (jnp.sum(complete, axis=1) / query_tokens).reshape(shard_total, capacity)
    returned = lax.all_to_all(pair_scores, "shard", split_axis=0, concat_axis=0, tiled=True)
    pair_rows = jnp.take(passage_row, candidates.reshape(-1), axis=0)
    owners = pair_rows // passage_count
    onehot = (owners[:, None] == jnp.arange(shard_total, dtype=jnp.int32)[None, :]).astype(
        jnp.int32
    )
    ranking = jnp.sum((jnp.cumsum(onehot, axis=0) - onehot) * onehot, axis=1)
    my_places = owners * capacity + ranking
    scores = jnp.take(returned.reshape(-1), my_places, axis=0).reshape(query_count, per_query)
    return (token_best, scores)


def solution(mesh):
    in_specs = (
        P("shard", None, None),
        P(("shard", "cent"), None),
        P("shard", "cent", None),
        P("shard"),
        P(),
        P("shard", None),
    )
    out_specs = (P("shard", None), P("shard", None))
    return jax.shard_map(
        per_device, mesh=mesh, in_specs=in_specs, out_specs=out_specs, check_vma=False
    )
```

profile of v0, /device:TPU:1, one launch (start us, length us, event | category | flops | bytes accessed | tf_op | source)
XLA Modules:
  0.0 415.2 jit_solution(12105765791642082866)
XLA Ops:
  7.9 0.8 reshape.445
  8.7 0.8 reshape.447
  9.5 0.8 reshape.446
  10.3 55.1 %all_gather.7 = s32[1024,16]{1,0:T(8,128)S(1)} all-gather(s32[16,16]{1,0:T(8,128)} %param.11), channel_id=1, replica_groups=mesh['shard'=64,'cent'=4] {'shard'}, dimensions={0}, use_global_device_ids=true | all-gather | bytes 66560 | tf_op jit(solution)/shard_map/all_gather | solution.py:21
  66.0 2.1 gather_fusion.4
  69.3 90.5 %gather_fusion = s32[16384]{0:T(1024)S(1)} fusion(s32[16384]{0:T(1024)S(1)} %copy-done.1, s32[16384]{0:T(1024)S(1)} %broadcast_clamp_fusion), kind=kCustom, calls=%fused_computation | custom fusion | bytes 196608 | tf_op jit(solution)/shard_map/jit(_take)/gather | solution.py:27
  161.5 60.3 %scatter_custom_fusion.1 = s32[768]{0:T(1024)S(1)} fusion(s32[16384]{0:T(1024)S(1)} %bitcast.49, s32[16384]{0:T(1024)S(1)} %add_select_fusion, s32[]{:T(128)} %constant.143.clone.1), kind=kCustom, calls=%fused_computation.97 | custom fusion | bytes 3076 | tf_op jit(solution)/shard_map/scatter | solution.py:40
  221.8 60.5 %scatter_custom_fusion = s32[768]{0:T(1024)S(1)} fusion(s32[16384]{0:T(1024)S(1)} %bitcast.50, s32[16384]{0:T(1024)S(1)} %add_select_fusion.1, s32[]{:T(128)} %constant.143.clone.1), kind=kCustom, calls=%fused_computation.99 | custom fusion | bytes 3076 | tf_op jit(solution)/shard_map/scatter | solution.py:37
  282.3 5.0 %gather_fusion.1 = s32[768]{0:T(1024)S(1)} fusion(s32[256]{0:T(256)S(1)} %copy-done.2, s32[1024]{0:T(1024)S(1)} %pad_clamp_fusion.3), kind=kCustom, calls=%fused_computation.1 | custom fusion | bytes 9216 | tf_op jit(solution)/shard_map/jit(_take)/gather | solution.py:46
  287.4 4.5 %gather_fusion.3 = bf16[768,32,128]{2,1,0:T(8,128)(2,1)} fusion(bf16[256,32,128]{2,1,0:T(8,128)(2,1)S(1)} %copy-done, s32[1024]{0:T(1024)S(1)} %pad_clamp_fusion.3), kind=kCustom, calls=%fused_computation.3 | custom fusion | bytes 12585984 | tf_op jit(solution)/shard_map/jit(_take)/gather | solution.py:43
  292.3 17.0 %convolution_reduce_fusion = f32[32768]{0:T(1024)S(1)} fusion(bf16[32768,128]{1,0:T(8,128)(2,1)} %bitcast.43, bf16[768,128]{1,0:T(8,128)(2,1)S(1)} %copy-done.5), kind=kOutput, calls=%fused_computation.8 | convolution fusion | flops 6467584000 | bytes 8716288 | tf_op jit(solution)/shard_map/rd,cd->rc/dot_general | solution.py:23
  309.5 0.9 reshape.532
  310.4 6.4 %all-to-all-start = ((f32[64,1,512]{2,1,0:T(1,128)}), f32[64,1,512]{2,1,0:T(1,128)S(1)}, u32[]{:S(2)}, u32[]{:S(2)}) async-start(f32[64,1,512]{2,1,0:T(1,128)} %reshape.532), calls=%async_computation | async-start | bytes 262144 | tf_op jit(solution)/shard_map/all_to_all | solution.py:25
  316.9 8.3 %gather_fusion.2 = bf16[768,32,128]{2,1,0:T(8,128)(2,1)} fusion(bf16[1024,32,128]{2,1,0:T(8,128)(2,1)} %all-gather.2.cloned.1.call-done, s32[1024]{0:T(1024)S(1)} %pad_clamp_fusion.2), kind=kCustom, calls=%fused_computation.2 | custom fusion | bytes 12585984 | tf_op jit(solution)/shard_map/jit(_take)/gather | solution.py:42
  325.2 8.3 %select_reduce_fusion = f32[768,32]{1,0:T(8,128)S(1)} fusion(pred[768,32]{1,0:T(8,128)(4,1)S(1)} %broadcast_compare_fusion, bf16[768,32,128]{2,1,0:T(8,128)(2,1)} %gather_fusion.3, pred[768]{0:T(1024)(128)(4,1)S(1)} %get-tuple-element.9, bf16[768,32,128]{2,1,0:T(8,128)(2,1)} %gather_fusion.2, pred[768]{0:T(1024)(128)(4,1)S(1)} %compare_and_fusion), kind=kOutput, calls=%fused_computation.9 | convolution fusion | flops 209166336 | bytes 12707328 | tf_op jit(solution)/shard_map/ntd,npd->ntp/dot_general | solution.py:44
  334.1 1.0 reduce.8
  335.4 0.7 pad_maximum_fusion
  336.2 44.7 %all-reduce.2.cloned.1.call-done = f32[784,32]{0,1:T(8,128)} async-done(((f32[784,32]{0,1:T(8,128)}), f32[784,32]{0,1:T(8,128)}) %all-reduce.2.cloned.1.call-update) | async-done | bytes 100368 | tf_op jit(solution)/shard_map/pmax | solution.py:49
  381.0 1.0 slice_reduce_fusion
  382.7 12.9 %all-to-all-start.1 = ((f32[64,1,12]{2,1,0:T(1,128)}), f32[64,1,12]{2,1,0:T(1,128)S(1)}, u32[]{:S(2)}, u32[]{:S(2)}) async-start(f32[64,1,12]{2,1,0:T(1,128)} %bitcast.9), calls=%async_computation.1 | async-start | bytes 65536 | tf_op jit(solution)/shard_map/all_to_all | solution.py:53
  395.7 0.7 slice.37
  397.1 7.7 %all-to-all-done.1 = f32[64,1,12]{2,1,0:T(1,128)S(1)} async-done(((f32[64,1,12]{2,1,0:T(1,128)}), f32[64,1,12]{2,1,0:T(1,128)S(1)}, u32[]{:S(2)}, u32[]{:S(2)}) %all-to-all-start.1) | async-done | bytes 3104 | tf_op jit(solution)/shard_map/all_to_all | solution.py:53
  405.4 0.7 reduce.7
  406.2 1.4 gather_fusion.5
  (72 shorter events, 8.6 us)
Async XLA Ops:
  7.2 280.2 %copy-start = (bf16[256,32,128]{2,1,0:T(8,128)(2,1)S(1)}, bf16[256,32,128]{2,1,0:T(8,128)(2,1)}, u32[]{:S(2)}) copy-start(bf16[256,32,128]{2,1,0:T(8,128)(2,1)} %param.8) | copy-start | bytes 6291460
  7.2 62.1 %copy-start.1 = (s32[16384]{0:T(1024)S(1)}, s32[16384]{0:T(1024)}, u32[]{:S(2)}) copy-start(s32[16384]{0:T(1024)} %param.10) | copy-start | bytes 196612
  7.2 285.1 %all-gather.2.cloned.1.call-start = ((), (), s32[]{:S(2)}) async-start(), calls=%async_computation.2 | async-start | bytes 8519680 | tf_op jit(solution)/shard_map/all_gather | solution.py:20
  69.0 90.8 %copy-start.4 = (s32[64,3]{0,1:T(4,128)}, s32[64,3]{0,1:T(4,128)S(1)}, u32[]{:S(2)}) copy-start(s32[64,3]{0,1:T(4,128)S(1)} %reduce-window.19) | copy-start | bytes 2308
  69.2 213.1 %copy-start.2 = (s32[256]{0:T(256)S(1)}, s32[256]{0:T(256)}, u32[]{:S(2)}) copy-start(s32[256]{0:T(256)} %param.9) | copy-start | bytes 3076
  287.3 4.6 %slice-start = ((s32[64,3]{0,1:T(4,128)}), s32[64,2]{0,1:T(2,128)S(1)}, s32[]{:S(2)}) async-start(s32[64,3]{0,1:T(4,128)} %copy-done.4), calls=%async_computation.4 | async-start | bytes 2048 | tf_op jit(solution)/shard_map/slice.5
  287.4 4.9 %copy-start.5 = (bf16[768,128]{1,0:T(8,128)(2,1)S(1)}, bf16[768,128]{1,0:T(8,128)(2,1)}, u32[]{:S(2)}) copy-start(bf16[768,128]{1,0:T(8,128)(2,1)} %param.7) | copy-start | bytes 589828
  310.4 23.2 %all-to-all-start = ((f32[64,1,512]{2,1,0:T(1,128)}), f32[64,1,512]{2,1,0:T(1,128)S(1)}, u32[]{:S(2)}, u32[]{:S(2)}) async-start(f32[64,1,512]{2,1,0:T(1,128)} %reshape.532), calls=%async_computation | async-start | bytes 262144 | tf_op jit(solution)/shard_map/all_to_all | solution.py:25
  316.8 64.1 %all-reduce.2.cloned.1.call-start = ((), (), s32[]{:S(2)}) async-start(), calls=%async_computation.3 | async-start | bytes 229376 | tf_op jit(solution)/shard_map/pmax | solution.py:49
  325.2 82.5 %copy-start.3 = (s32[16,16]{1,0:T(8,128)S(1)}, s32[16,16]{1,0:T(8,128)}, u32[]{:S(2)}) copy-start(s32[16,16]{1,0:T(8,128)} %param.11) | copy-start | bytes 3076
  382.7 22.2 %all-to-all-start.1 = ((f32[64,1,12]{2,1,0:T(1,128)}), f32[64,1,12]{2,1,0:T(1,128)S(1)}, u32[]{:S(2)}, u32[]{:S(2)}) async-start(f32[64,1,12]{2,1,0:T(1,128)} %bitcast.9), calls=%async_computation.1 | async-start | bytes 65536 | tf_op jit(solution)/shard_map/all_to_all | solution.py:53
Sparse Core Ops, SparseCore 0:
  10.8 87.3 all-gather.1
  336.3 44.5 all-reduce.1
where the time goes:
time: 416 us; the launch traced here: 415 us
  local copies, waits for them, and re-layouts  241 us (58%)
  blocking collectives  55.1 us (13%)
  waiting for transfers between devices  53.2 us (13%)
  matrix products  25.3 us (6%)
  starting transfers between devices  19.4 us (5%)
  between operations  14.4 us (3%)
  other arithmetic  6.63 us (2%)
    gather x1, local copies, waits for them, and re-layouts, per_device(): all_rows = jnp.take(passage_row, cand_block.reshape(-1), axis=0)  90.5 us
    scatter x1, local copies, waits for them, and re-layouts, per_device(): slot_table = jnp.zeros((shard_total * capacity,), jnp.int32).at[places].s...  60.5 us
    scatter x1, local copies, waits for them, and re-layouts, per_device(): jnp.zeros((shard_total * capacity,), jnp.int32).at[places]  60.3 us
    all_gather x1, blocking collectives, per_device(): cand_block = lax.all_gather(candidates, 'shard', axis=0, tiled=True)  55.1 us
    pmax x1, waiting for transfers between devices, per_device(): lax.pmax(jnp.concatenate([shard_best, partial_value], axis=0), 'cent')  44.7 us
    dot_general x1, matrix products, per_device(): jnp.einsum('rd,cd->rc', flattened, centroids, preferred_element_type=jnp....  17 us
    all_to_all x1, starting transfers between devices, per_device(): lax.all_to_all(pair_scores, 'shard', split_axis=0, concat_axis=0, tiled=T...  12.9 us
  transfers between devices with their start and end apart: 4, of which 2 were waited for; matrix products, arithmetic and copies ran while one was open for 60% of the time, Pallas kernels for 0%

commit v1 on v0

--- a/solution.py
+++ b/solution.py
@@ -4,6 +4,17 @@
 from jax.sharding import PartitionSpec as P
 
 masked_score = -1e30
+
+
+def recast_heads_over_axis(panel):
+    wide_n = lax.axis_size("shard")
+    return lax.all_to_all(
+        jnp.tile(panel, list(map(lambda src_i: wide_n if src_i == 0 else 1, range(panel.ndim)))),
+        "shard",
+        split_axis=0,
+        tiled=True,
+        concat_axis=0,
+    )
 
 
 def per_device(queries, centroids, passages, lengths, passage_row, candidates):
@@ -18,7 +29,7 @@
     pairs_here = query_count * per_query
     my_shard = lax.axis_index("shard")
     query_block = lax.all_gather(queries, "shard", axis=0, tiled=True)
-    cand_block = lax.all_gather(candidates, "shard", axis=0, tiled=True)
+    cand_block = recast_heads_over_axis(candidates)
     flattened = query_block.reshape(-1, feature_width)
     scored = jnp.einsum("rd,cd->rc", flattened, centroids, preferred_element_type=jnp.float32)
     local_best = jnp.max(scored, axis=1).reshape(shard_total, query_count, query_tokens)

time: 416 us -> 381 us (0.916)
  blocking collectives: 55.1 us -> 0 us
  starting transfers between devices: 19.4 us -> 32.3 us
  waiting for transfers between devices: 53.2 us -> 57.4 us
    all_gather x1 -> x0, blocking collectives: 55.1 us -> none  [per_device(): cand_block = lax.all_gather(candidates, 'shard', axis=0, tiled=True)]
    all_to_all x0 -> x1, starting transfers between devices: none -> 13.1 us  [recast_heads_over_axis(): lax.all_to_all(jnp.tile(panel, list(map(lambda src_i: wide_n if src_i ==...]
  transfers between devices with their start and end apart: 4 -> 5, of which waited for: 2 -> 3; matrix products, arithmetic and copies ran while one was open for 60% -> 66% of each run, Pallas kernels for 0% -> 0%
where the time goes in v1:
time: 381 us; the launch traced here: 380 us
  local copies, waits for them, and re-layouts  243 us (64%)
  waiting for transfers between devices  57.4 us (15%)
  starting transfers between devices  32.3 us (8%)
  matrix products  25.3 us (7%)
  between operations  14.4 us (4%)
  other arithmetic  7.43 us (2%)
    gather x1, local copies, waits for them, and re-layouts, per_device(): all_rows = jnp.take(passage_row, cand_block.reshape(-1), axis=0)  90.5 us
    scatter x1, local copies, waits for them, and re-layouts, per_device(): slot_table = jnp.zeros((shard_total * capacity,), jnp.int32).at[places].s...  60.5 us
    scatter x1, local copies, waits for them, and re-layouts, per_device(): jnp.zeros((shard_total * capacity,), jnp.int32).at[places]  60.3 us
    pmax x1, waiting for transfers between devices, per_device(): lax.pmax(jnp.concatenate([shard_best, partial_value], axis=0), 'cent')  44.7 us
    dot_general x1, matrix products, per_device(): jnp.einsum('rd,cd->rc', flattened, centroids, preferred_element_type=jnp....  17 us
    all_to_all x1, starting transfers between devices, recast_heads_over_axis(): lax.all_to_all(jnp.tile(panel, list(map(lambda src_i: wide_n if src_i ==...  13.1 us
    all_to_all x1, starting transfers between devices, per_device(): lax.all_to_all(pair_scores, 'shard', split_axis=0, concat_axis=0, tiled=T...  12.9 us
    gather x1, local copies, waits for them, and re-layouts, per_device(): asked = jnp.take(query_block, query_table, axis=0)  8.3 us
  transfers between devices with their start and end apart: 5, of which 3 were waited for; matrix products, arithmetic and copies ran while one was open for 66% of the time, Pallas kernels for 0%

profile of v1, /device:TPU:1, one launch (start us, length us, event | category | flops | bytes accessed | tf_op | source)
XLA Modules:
  0.0 380.3 jit_solution(4466139559782979723)
XLA Ops:
  8.7 0.9 reshape.543
  9.5 13.1 %all-to-all-start.1 = ((s32[64,1,256]{2,1,0:T(1,128)}), s32[64,1,256]{2,1,0:T(1,128)S(1)}, u32[]{:S(2)}, u32[]{:S(2)}) async-start(s32[64,1,256]{2,1,0:T(1,128)} %reshape.543), calls=%async_computation.1 | async-start | bytes 131072 | tf_op jit(solution)/shard_map/all_to_all | solution.py:11
  22.7 0.8 reshape.456
  23.5 0.8 reshape.458
  24.2 0.8 reshape.457
  25.0 2.1 gather_fusion.4
  28.3 4.2 %all-to-all-done.1 = s32[64,1,256]{2,1,0:T(1,128)S(1)} async-done(((s32[64,1,256]{2,1,0:T(1,128)}), s32[64,1,256]{2,1,0:T(1,128)S(1)}, u32[]{:S(2)}, u32[]{:S(2)}) %all-to-all-start.1) | async-done | bytes 65568 | tf_op jit(solution)/shard_map/all_to_all | solution.py:11
  32.9 0.8 reduce.8
  34.8 90.5 %gather_fusion = s32[16384]{0:T(1024)S(1)} fusion(s32[16384]{0:T(1024)S(1)} %copy-done.1, s32[16384]{0:T(1024)S(1)} %broadcast_clamp_fusion), kind=kCustom, calls=%fused_computation | custom fusion | bytes 196608 | tf_op jit(solution)/shard_map/jit(_take)/gather | solution.py:38
  127.0 60.3 %scatter_custom_fusion.1 = s32[768]{0:T(1024)S(1)} fusion(s32[16384]{0:T(1024)S(1)} %bitcast.51, s32[16384]{0:T(1024)S(1)} %add_select_fusion, s32[]{:T(128)} %constant.143.clone.1), kind=kCustom, calls=%fused_computation.97 | custom fusion | bytes 3076 | tf_op jit(solution)/shard_map/scatter | solution.py:51
  187.4 60.5 %scatter_custom_fusion = s32[768]{0:T(1024)S(1)} fusion(s32[16384]{0:T(1024)S(1)} %bitcast.52, s32[16384]{0:T(1024)S(1)} %add_select_fusion.1, s32[]{:T(128)} %constant.143.clone.1), kind=kCustom, calls=%fused_computation.99 | custom fusion | bytes 3076 | tf_op jit(solution)/shard_map/scatter | solution.py:48
  247.9 5.0 %gather_fusion.1 = s32[768]{0:T(1024)S(1)} fusion(s32[256]{0:T(256)S(1)} %copy-done.2, s32[1024]{0:T(1024)S(1)} %pad_clamp_fusion.3), kind=kCustom, calls=%fused_computation.1 | custom fusion | bytes 9216 | tf_op jit(solution)/shard_map/jit(_take)/gather | solution.py:57
  252.9 4.5 %gather_fusion.3 = bf16[768,32,128]{2,1,0:T(8,128)(2,1)} fusion(bf16[256,32,128]{2,1,0:T(8,128)(2,1)S(1)} %copy-done, s32[1024]{0:T(1024)S(1)} %pad_clamp_fusion.3), kind=kCustom, calls=%fused_computation.3 | custom fusion | bytes 12585984 | tf_op jit(solution)/shard_map/jit(_take)/gather | solution.py:54
  257.7 17.0 %convolution_reduce_fusion = f32[32768]{0:T(1024)S(1)} fusion(bf16[32768,128]{1,0:T(8,128)(2,1)} %bitcast.44, bf16[768,128]{1,0:T(8,128)(2,1)S(1)} %copy-done.4), kind=kOutput, calls=%fused_computation.8 | convolution fusion | flops 6467584000 | bytes 8716288 | tf_op jit(solution)/shard_map/rd,cd->rc/dot_general | solution.py:34
  274.9 0.9 reshape.545
  275.8 6.2 %all-to-all-start = ((f32[64,1,512]{2,1,0:T(1,128)}), f32[64,1,512]{2,1,0:T(1,128)S(1)}, u32[]{:S(2)}, u32[]{:S(2)}) async-start(f32[64,1,512]{2,1,0:T(1,128)} %reshape.545), calls=%async_computation | async-start | bytes 262144 | tf_op jit(solution)/shard_map/all_to_all | solution.py:36
  282.0 8.3 %gather_fusion.2 = bf16[768,32,128]{2,1,0:T(8,128)(2,1)} fusion(bf16[1024,32,128]{2,1,0:T(8,128)(2,1)} %all-gather.2.cloned.1.call-done, s32[1024]{0:T(1024)S(1)} %pad_clamp_fusion.2), kind=kCustom, calls=%fused_computation.2 | custom fusion | bytes 12585984 | tf_op jit(solution)/shard_map/jit(_take)/gather | solution.py:53
  290.3 8.3 %select_reduce_fusion = f32[768,32]{1,0:T(8,128)S(1)} fusion(pred[768,32]{1,0:T(8,128)(4,1)S(1)} %broadcast_compare_fusion, bf16[768,32,128]{2,1,0:T(8,128)(2,1)} %gather_fusion.3, pred[768]{0:T(1024)(128)(4,1)S(1)} %get-tuple-element.9, bf16[768,32,128]{2,1,0:T(8,128)(2,1)} %gather_fusion.2, pred[768]{0:T(1024)(128)(4,1)S(1)} %compare_and_fusion), kind=kOutput, calls=%fused_computation.9 | convolution fusion | flops 209166336 | bytes 12707328 | tf_op jit(solution)/shard_map/ntd,npd->ntp/dot_general | solution.py:55
  299.3 1.0 reduce.9
  301.4 44.7 %all-reduce.2.cloned.1.call-done = f32[784,32]{0,1:T(8,128)} async-done(((f32[784,32]{0,1:T(8,128)}), f32[784,32]{0,1:T(8,128)}) %all-reduce.2.cloned.1.call-update) | async-done | bytes 100368 | tf_op jit(solution)/shard_map/pmax | solution.py:60
  346.1 1.0 slice_reduce_fusion
  347.8 12.9 %all-to-all-start.2 = ((f32[64,1,12]{2,1,0:T(1,128)}), f32[64,1,12]{2,1,0:T(1,128)S(1)}, u32[]{:S(2)}, u32[]{:S(2)}) async-start(f32[64,1,12]{2,1,0:T(1,128)} %bitcast.10), calls=%async_computation.2 | async-start | bytes 65536 | tf_op jit(solution)/shard_map/all_to_all | solution.py:64
  362.3 7.7 %all-to-all-done.2 = f32[64,1,12]{2,1,0:T(1,128)S(1)} async-done(((f32[64,1,12]{2,1,0:T(1,128)}), f32[64,1,12]{2,1,0:T(1,128)S(1)}, u32[]{:S(2)}, u32[]{:S(2)}) %all-to-all-start.2) | async-done | bytes 3104 | tf_op jit(solution)/shard_map/all_to_all | solution.py:64
  371.4 1.4 gather_fusion.5
  (76 shorter events, 12.3 us)
Async XLA Ops:
  7.2 245.7 %copy-start = (bf16[256,32,128]{2,1,0:T(8,128)(2,1)S(1)}, bf16[256,32,128]{2,1,0:T(8,128)(2,1)}, u32[]{:S(2)}) copy-start(bf16[256,32,128]{2,1,0:T(8,128)(2,1)} %param.8) | copy-start | bytes 6291460
  7.2 27.6 %copy-start.1 = (s32[16384]{0:T(1024)S(1)}, s32[16384]{0:T(1024)}, u32[]{:S(2)}) copy-start(s32[16384]{0:T(1024)} %param.10) | copy-start | bytes 196612
  7.2 250.5 %all-gather.2.cloned.1.call-start = ((), (), s32[]{:S(2)}) async-start(), calls=%async_computation.3 | async-start | bytes 8519680 | tf_op jit(solution)/shard_map/all_gather | solution.py:31
  9.5 22.9 %all-to-all-start.1 = ((s32[64,1,256]{2,1,0:T(1,128)}), s32[64,1,256]{2,1,0:T(1,128)S(1)}, u32[]{:S(2)}, u32[]{:S(2)}) async-start(s32[64,1,256]{2,1,0:T(1,128)} %reshape.543), calls=%async_computation.1 | async-start | bytes 131072 | tf_op jit(solution)/shard_map/all_to_all | solution.py:11
  34.7 213.1 %copy-start.2 = (s32[256]{0:T(256)S(1)}, s32[256]{0:T(256)}, u32[]{:S(2)}) copy-start(s32[256]{0:T(256)} %param.9) | copy-start | bytes 3076
  252.9 4.8 %copy-start.4 = (bf16[768,128]{1,0:T(8,128)(2,1)S(1)}, bf16[768,128]{1,0:T(8,128)(2,1)}, u32[]{:S(2)}) copy-start(bf16[768,128]{1,0:T(8,128)(2,1)} %param.7) | copy-start | bytes 589828
  275.8 23.0 %all-to-all-start = ((f32[64,1,512]{2,1,0:T(1,128)}), f32[64,1,512]{2,1,0:T(1,128)S(1)}, u32[]{:S(2)}, u32[]{:S(2)}) async-start(f32[64,1,512]{2,1,0:T(1,128)} %reshape.545), calls=%async_computation | async-start | bytes 262144 | tf_op jit(solution)/shard_map/all_to_all | solution.py:36
  282.0 64.1 %all-reduce.2.cloned.1.call-start = ((), (), s32[]{:S(2)}) async-start(), calls=%async_computation.4 | async-start | bytes 229376 | tf_op jit(solution)/shard_map/pmax | solution.py:60
  290.3 82.5 %copy-start.3 = (s32[16,16]{1,0:T(8,128)S(1)}, s32[16,16]{1,0:T(8,128)}, u32[]{:S(2)}) copy-start(s32[16,16]{1,0:T(8,128)} %param.11) | copy-start | bytes 3076
  347.8 22.2 %all-to-all-start.2 = ((f32[64,1,12]{2,1,0:T(1,128)}), f32[64,1,12]{2,1,0:T(1,128)S(1)}, u32[]{:S(2)}, u32[]{:S(2)}) async-start(f32[64,1,12]{2,1,0:T(1,128)} %bitcast.10), calls=%async_computation.2 | async-start | bytes 65536 | tf_op jit(solution)/shard_map/all_to_all | solution.py:64
Sparse Core Ops, SparseCore 0:
  10.8 87.2 all-gather.1
  301.5 44.5 all-reduce.1
